TPU v7x, 128 devices: a whole 4x4x4 slice. The times are simulated.
128 devices in a mesh: tm: 32 (over x, z, core), chan: 4 (over y).
Axes of the slice: x: 4, y: 4, z: 4, core: 2. Of those that a mesh axis runs over, the one named last changes fastest.
Arguments:
- inputs: bfloat16 [64, 256, 512], P('tm'), may hold values from -6 to 6
- decay: float32 [64, 512], P('tm', 'chan'), may hold values from 0 to 1, as said below
- kernel_b: bfloat16 [9, 512, 256], P(None, 'chan'), may hold values from -0.125 to 0.125
- kernel_c: bfloat16 [9, 256, 512], P(None, 'chan'), may hold values from -0.09375 to 0.09375
- cotangent: bfloat16 [64, 256, 512], P('tm', 'chan'), may hold values from -0.03125 to 0.03125
Outputs:
- grad_b: float32 [9, 512, 256], P(None, 'chan')
- grad_c: float32 [9, 256, 512], P(None, 'chan')
- decay_grad: float32 [64, 512], P('tm', 'chan')
Inputs may be any that keep to these rules, and one draw needn't show every extreme that they name: decay lies strictly between 0 and 1.
All inputs are finite; a program needn't handle non-finite values.
Results may differ from a plain program's by a relative error of at most 0.003.
Values may be sent and summed in bfloat16 or wider, within the bound.
No kernel may reach another device: no remote copies, remote signals or barrier semaphores. Data moves between devices by JAX's collectives and lax.ppermute only.
A program may use at most 128 MiB of HBM per device.

v0:
```python
import jax
import jax.numpy as jnp
from jax import lax
from jax.sharding import PartitionSpec as P

W = 64
offsets = ((-1, -1), (-1, 0), (-1, 1), (0, -1), (0, 0), (0, 1), (1, -1), (1, 0), (1, 1))


def passed_along(value, axis, steps):
    count = lax.axis_size(axis)
    first, last = (max(0, -steps), min(count, count - steps))
    return lax.ppermute(value, axis, [(source, source + steps) for source in range(first, last)])


def shift_cells(source, row_shift, col_shift, grid_width):
    cell_count = source.shape[-1]
    margin = grid_width + 1
    padded = jnp.pad(source, [(0, 0)] * (source.ndim - 1) + [(margin, margin)])
    first_cell = margin + row_shift * grid_width + col_shift
    shifted = lax.slice_in_dim(padded, first_cell, first_cell + cell_count, axis=source.ndim - 1)
    column = jnp.arange(cell_count) % grid_width
    inside = (column + col_shift >= 0) & (column + col_shift < grid_width)
    return jnp.where(inside, shifted, jnp.zeros((), source.dtype))


def stencil_stack(source, grid_width, decay_factor):
    parts = [
        shift_cells(source, decay_factor * pair[0], decay_factor * pair[1], grid_width)
        for pair in offsets
    ]
    return jnp.stack(parts, axis=source.ndim - 2)


def body(inputs, decay, kernel_b, kernel_c, cotangent):
    local_rows = kernel_b.shape[1]
    cell_count = inputs.shape[-1]
    blank_state = jnp.zeros((local_rows, cell_count), jnp.float32)
    input_stack = stencil_stack(inputs, W, 1)
    drives = jnp.einsum("kpc,fkcs->fps", kernel_b, input_stack, preferred_element_type=jnp.float32)

    def advance(current, frame_pair):
        frame_rate, drive = frame_pair
        current = frame_rate[:, None] * current + drive
        return (current, current)

    local_end, local_states = lax.scan(advance, blank_state, (decay, drives))
    decay_total = jnp.prod(decay, axis=0)

    def relay_state(turn_index, carried):
        outgoing = decay_total[:, None] * carried + local_end
        return passed_along(outgoing, "tm", 1)

    entering = lax.fori_loop(0, lax.axis_size("tm") - 1, relay_state, blank_state)
    cumulative = jnp.cumprod(decay, axis=0)
    states = local_states + cumulative[:, :, None] * entering[None]
    previous = jnp.concatenate([entering[None], states[:-1]], axis=0)
    states_bf = states.astype(jnp.bfloat16)
    cot_stack = stencil_stack(cotangent, W, -1)
    injected = lax.psum_scatter(
        jnp.einsum("kup,fkus->pfs", kernel_c, cot_stack, preferred_element_type=jnp.float32),
        "chan",
        scatter_dimension=0,
        tiled=True,
    )
    injected = jnp.moveaxis(injected, 1, 0)

    def retreat(carried, frame_pair):
        frame_rate, source = frame_pair
        adjoint = source + carried
        return (frame_rate[:, None] * adjoint, adjoint)

    message, local_adjoint = lax.scan(retreat, blank_state, (decay, injected), reverse=True)

    def relay_adjoint(turn_index, carried):
        outgoing = decay_total[:, None] * carried + message
        return passed_along(outgoing, "tm", -1)

    arriving = lax.fori_loop(0, lax.axis_size("tm") - 1, relay_adjoint, blank_state)
    suffix = jnp.flip(jnp.cumprod(jnp.flip(decay, 0), 0), 0)
    later_decay = jnp.concatenate([suffix[1:], jnp.ones_like(decay[:1])], axis=0)
    adjoint = local_adjoint + later_decay[:, :, None] * arriving[None]
    decay_grad = jnp.sum(adjoint * previous, axis=2)
    adjoint_bf = adjoint.astype(jnp.bfloat16)
    grad_b_part = jnp.einsum(
        "fps,fkcs->kpc", adjoint_bf, input_stack, preferred_element_type=jnp.float32
    )
    shifted = stencil_stack(lax.all_gather(states_bf, "chan", axis=1, tiled=True), W, 1)
    grad_c_part = jnp.einsum(
        "fus,fkps->kup", cotangent, shifted, preferred_element_type=jnp.float32
    )
    grad_b, grad_c = lax.psum((grad_b_part, grad_c_part), "tm")
    return (grad_b, grad_c, decay_grad)


def solution(mesh):
    in_specs = (
        P("tm", None, None),
        P("tm", "chan"),
        P(None, "chan", None),
        P(None, "chan", None),
        P("tm", "chan", None),
    )
    out_specs = (P(None, "chan", None), P(None, "chan", None), P("tm", "chan"))
    return jax.shard_map(body, mesh=mesh, in_specs=in_specs, out_specs=out_specs, check_vma=False)
```

profile of v0, /device:TPU:1, one launch (start us, length us, event | category | flops | bytes accessed | tf_op | source)
XLA Modules:
  0.0 817.5 jit_solution(8985757919530302460)
XLA Ops:
  20.7 275.2 %while.51 = (s32[]{:T(128)}, f32[128,512]{1,0:T(8,128)S(1)}, f32[128]{0:T(128)S(1)}, f32[128,512]{1,0:T(8,128)S(1)}, s32[]{:T(128)}) while((s32[]{:T(128)}, f32[128,512]{1,0:T(8,128)S(1)}, f32[128]{0:T(128)S(1)}, f32[128,512]{1,0:T(8,128)S(1)}, s32[]{:T(128)}) %tuple.101), condition=%wide.region_12.13_spmd, body=%wide.region_11.12_spmd.sunk | while | flops 131074 | bytes 1835621 | solution.py:54
  138.1 6.0 collective-permute-start.1
  147.5 6.5 collective-permute-start.1
  157.4 6.5 collective-permute-start.1
  167.3 6.5 collective-permute-start.1
  177.2 6.5 collective-permute-start.1
  187.1 6.5 collective-permute-start.1
  197.0 6.5 collective-permute-start.1
  206.9 6.5 collective-permute-start.1
  216.8 6.5 collective-permute-start.1
  226.7 6.5 collective-permute-start.1
  236.6 6.5 collective-permute-start.1
  246.5 6.5 collective-permute-start.1
  256.4 6.5 collective-permute-start.1
  266.3 6.5 collective-permute-start.1
  276.2 6.5 collective-permute-start.1
  286.1 6.5 collective-permute-start.1
  300.5 49.7 %all-gather.2.cloned.1.call-done = bf16[2,512,512]{2,1,0:T(8,128)(2,1)} async-done(((bf16[2,128,512]{2,1,0:T(8,128)(2,1)}), bf16[2,512,512]{2,1,0:T(8,128)(2,1)}) %all-gather.2.cloned.1.call-update) | async-done | bytes 1048592 | tf_op jit(solution)/shard_map/all_gather | solution.py:88
  361.1 23.6 %reduce-scatter.2.cloned.1.call-done = f32[128,2,512]{0,2,1:T(8,128)} async-done(((f32[512,2,512]{0,2,1:T(8,128)}), f32[128,2,512]{0,2,1:T(8,128)}) %reduce-scatter.2.cloned.1.call-update) | async-done | bytes 524304 | tf_op jit(solution)/shard_map/reduce_scatter | solution.py:60
  387.4 279.4 %while.50 = (s32[]{:T(128)}, f32[128,512]{1,0:T(8,128)S(1)}, f32[128]{0:T(128)S(1)}, f32[128,512]{1,0:T(8,128)S(1)}, s32[]{:T(128)}) while((s32[]{:T(128)}, f32[128,512]{1,0:T(8,128)S(1)}, f32[128]{0:T(128)S(1)}, f32[128,512]{1,0:T(8,128)S(1)}, s32[]{:T(128)}) %tuple.113), condition=%wide.region_6.7_spmd, body=%wide.region_5.6_spmd.sunk | while | flops 131074 | bytes 1835621 | solution.py:79
  397.4 5.8 collective-permute-done
  405.2 5.8 collective-permute-done
  413.0 5.8 collective-permute-done
  420.8 5.8 collective-permute-done
  428.5 5.8 collective-permute-done
  436.3 5.8 collective-permute-done
  444.1 5.8 collective-permute-done
  451.9 5.8 collective-permute-done
  483.0 5.8 collective-permute-done
  490.8 7.7 collective-permute-done
  500.6 7.9 collective-permute-done
  510.5 7.9 collective-permute-done
  520.4 7.9 collective-permute-done
  530.3 7.9 collective-permute-done
  540.2 7.9 collective-permute-done
  550.0 7.9 collective-permute-done
  559.9 7.9 collective-permute-done
  569.8 7.9 collective-permute-done
  579.7 7.9 collective-permute-done
  589.6 7.9 collective-permute-done
  599.5 7.9 collective-permute-done
  609.4 7.9 collective-permute-done
  619.3 7.9 collective-permute-done
  629.2 7.9 collective-permute-done
  639.1 7.9 collective-permute-done
  649.0 7.9 collective-permute-done
  658.9 7.9 collective-permute-done
  672.4 133.6 %all-reduce.6.cloned.1.call-done = (f32[9,128,256]{1,2,0:T(8,128)}, f32[9,64,512]{2,1,0:T(8,128)}) async-done(((f32[9,128,256]{1,2,0:T(8,128)}, f32[9,64,512]{2,1,0:T(8,128)}), (f32[9,128,256]{1,2,0:T(8,128)}, f32[9,64,512]{2,1,0:T(8,128)})) %all-reduce.6.cloned.1.call-update) | async-done | bytes 2359312 | tf_op jit(solution)/shard_map/psum | solution.py:92
  (235 shorter events, 301.6 us)
Async XLA Ops:
  7.2 343.0 %all-gather.2.cloned.1.call-start = ((), (), s32[]{:S(2)}) async-start(), calls=%async_computation.2 | async-start | bytes 1310720 | tf_op jit(solution)/shard_map/all_gather | solution.py:88
  20.8 8.2 %collective-permute-start.1 = (f32[128,512]{1,0:T(8,128)S(1)}, f32[128,512]{1,0:T(8,128)S(1)}, u32[]{:S(2)}, u32[]{:S(2)}) collective-permute-start(f32[128,512]{1,0:T(8,128)S(1)} %multiply_add_fusion.8), channel_id=1, source_target_pairs={{0,4},{4,8},{8,12},{12,16},{16,20},{20,24},{24,28},{28,32},{32,36}... | collective-permute-start | bytes 786440 | tf_op jit(solution)/shard_map/while/body/eval_jaxpr/ppermute | solution.py:13
  29.1 7.7 collective-permute-start.1
  36.9 7.7 collective-permute-start.1
  44.7 7.7 collective-permute-start.1
  60.2 7.7 collective-permute-start.1
  68.0 7.7 collective-permute-start.1
  75.8 7.7 collective-permute-start.1
  83.6 7.7 collective-permute-start.1
  91.4 7.7 collective-permute-start.1
  99.2 7.7 collective-permute-start.1
  138.1 9.3 %collective-permute-start.1 = (f32[128,512]{1,0:T(8,128)S(1)}, f32[128,512]{1,0:T(8,128)S(1)}, u32[]{:S(2)}, u32[]{:S(2)}) collective-permute-start(f32[128,512]{1,0:T(8,128)S(1)} %multiply_add_fusion.8), channel_id=1, source_target_pairs={{0,4},{4,8},{8,12},{12,16},{16,20},{20,24},{24,28},{28,32},{32,36}... | collective-permute-start | bytes 786440 | tf_op jit(solution)/shard_map/while/body/eval_jaxpr/ppermute | solution.py:13
  147.5 9.8 %collective-permute-start.1 = (f32[128,512]{1,0:T(8,128)S(1)}, f32[128,512]{1,0:T(8,128)S(1)}, u32[]{:S(2)}, u32[]{:S(2)}) collective-permute-start(f32[128,512]{1,0:T(8,128)S(1)} %multiply_add_fusion.8), channel_id=1, source_target_pairs={{0,4},{4,8},{8,12},{12,16},{16,20},{20,24},{24,28},{28,32},{32,36}... | collective-permute-start | bytes 786440 | tf_op jit(solution)/shard_map/while/body/eval_jaxpr/ppermute | solution.py:13
  157.4 9.8 %collective-permute-start.1 = (f32[128,512]{1,0:T(8,128)S(1)}, f32[128,512]{1,0:T(8,128)S(1)}, u32[]{:S(2)}, u32[]{:S(2)}) collective-permute-start(f32[128,512]{1,0:T(8,128)S(1)} %multiply_add_fusion.8), channel_id=1, source_target_pairs={{0,4},{4,8},{8,12},{12,16},{16,20},{20,24},{24,28},{28,32},{32,36}... | collective-permute-start | bytes 786440 | tf_op jit(solution)/shard_map/while/body/eval_jaxpr/ppermute | solution.py:13
  167.3 9.8 %collective-permute-start.1 = (f32[128,512]{1,0:T(8,128)S(1)}, f32[128,512]{1,0:T(8,128)S(1)}, u32[]{:S(2)}, u32[]{:S(2)}) collective-permute-start(f32[128,512]{1,0:T(8,128)S(1)} %multiply_add_fusion.8), channel_id=1, source_target_pairs={{0,4},{4,8},{8,12},{12,16},{16,20},{20,24},{24,28},{28,32},{32,36}... | collective-permute-start | bytes 786440 | tf_op jit(solution)/shard_map/while/body/eval_jaxpr/ppermute | solution.py:13
  177.2 9.8 %collective-permute-start.1 = (f32[128,512]{1,0:T(8,128)S(1)}, f32[128,512]{1,0:T(8,128)S(1)}, u32[]{:S(2)}, u32[]{:S(2)}) collective-permute-start(f32[128,512]{1,0:T(8,128)S(1)} %multiply_add_fusion.8), channel_id=1, source_target_pairs={{0,4},{4,8},{8,12},{12,16},{16,20},{20,24},{24,28},{28,32},{32,36}... | collective-permute-start | bytes 786440 | tf_op jit(solution)/shard_map/while/body/eval_jaxpr/ppermute | solution.py:13
  187.1 9.8 %collective-permute-start.1 = (f32[128,512]{1,0:T(8,128)S(1)}, f32[128,512]{1,0:T(8,128)S(1)}, u32[]{:S(2)}, u32[]{:S(2)}) collective-permute-start(f32[128,512]{1,0:T(8,128)S(1)} %multiply_add_fusion.8), channel_id=1, source_target_pairs={{0,4},{4,8},{8,12},{12,16},{16,20},{20,24},{24,28},{28,32},{32,36}... | collective-permute-start | bytes 786440 | tf_op jit(solution)/shard_map/while/body/eval_jaxpr/ppermute | solution.py:13
  197.0 9.8 %collective-permute-start.1 = (f32[128,512]{1,0:T(8,128)S(1)}, f32[128,512]{1,0:T(8,128)S(1)}, u32[]{:S(2)}, u32[]{:S(2)}) collective-permute-start(f32[128,512]{1,0:T(8,128)S(1)} %multiply_add_fusion.8), channel_id=1, source_target_pairs={{0,4},{4,8},{8,12},{12,16},{16,20},{20,24},{24,28},{28,32},{32,36}... | collective-permute-start | bytes 786440 | tf_op jit(solution)/shard_map/while/body/eval_jaxpr/ppermute | solution.py:13
  206.9 9.8 %collective-permute-start.1 = (f32[128,512]{1,0:T(8,128)S(1)}, f32[128,512]{1,0:T(8,128)S(1)}, u32[]{:S(2)}, u32[]{:S(2)}) collective-permute-start(f32[128,512]{1,0:T(8,128)S(1)} %multiply_add_fusion.8), channel_id=1, source_target_pairs={{0,4},{4,8},{8,12},{12,16},{16,20},{20,24},{24,28},{28,32},{32,36}... | collective-permute-start | bytes 786440 | tf_op jit(solution)/shard_map/while/body/eval_jaxpr/ppermute | solution.py:13
  216.8 9.8 %collective-permute-start.1 = (f32[128,512]{1,0:T(8,128)S(1)}, f32[128,512]{1,0:T(8,128)S(1)}, u32[]{:S(2)}, u32[]{:S(2)}) collective-permute-start(f32[128,512]{1,0:T(8,128)S(1)} %multiply_add_fusion.8), channel_id=1, source_target_pairs={{0,4},{4,8},{8,12},{12,16},{16,20},{20,24},{24,28},{28,32},{32,36}... | collective-permute-start | bytes 786440 | tf_op jit(solution)/shard_map/while/body/eval_jaxpr/ppermute | solution.py:13
  226.7 9.8 %collective-permute-start.1 = (f32[128,512]{1,0:T(8,128)S(1)}, f32[128,512]{1,0:T(8,128)S(1)}, u32[]{:S(2)}, u32[]{:S(2)}) collective-permute-start(f32[128,512]{1,0:T(8,128)S(1)} %multiply_add_fusion.8), channel_id=1, source_target_pairs={{0,4},{4,8},{8,12},{12,16},{16,20},{20,24},{24,28},{28,32},{32,36}... | collective-permute-start | bytes 786440 | tf_op jit(solution)/shard_map/while/body/eval_jaxpr/ppermute | solution.py:13
  236.6 9.8 %collective-permute-start.1 = (f32[128,512]{1,0:T(8,128)S(1)}, f32[128,512]{1,0:T(8,128)S(1)}, u32[]{:S(2)}, u32[]{:S(2)}) collective-permute-start(f32[128,512]{1,0:T(8,128)S(1)} %multiply_add_fusion.8), channel_id=1, source_target_pairs={{0,4},{4,8},{8,12},{12,16},{16,20},{20,24},{24,28},{28,32},{32,36}... | collective-permute-start | bytes 786440 | tf_op jit(solution)/shard_map/while/body/eval_jaxpr/ppermute | solution.py:13
  246.5 9.8 %collective-permute-start.1 = (f32[128,512]{1,0:T(8,128)S(1)}, f32[128,512]{1,0:T(8,128)S(1)}, u32[]{:S(2)}, u32[]{:S(2)}) collective-permute-start(f32[128,512]{1,0:T(8,128)S(1)} %multiply_add_fusion.8), channel_id=1, source_target_pairs={{0,4},{4,8},{8,12},{12,16},{16,20},{20,24},{24,28},{28,32},{32,36}... | collective-permute-start | bytes 786440 | tf_op jit(solution)/shard_map/while/body/eval_jaxpr/ppermute | solution.py:13
  256.4 9.8 %collective-permute-start.1 = (f32[128,512]{1,0:T(8,128)S(1)}, f32[128,512]{1,0:T(8,128)S(1)}, u32[]{:S(2)}, u32[]{:S(2)}) collective-permute-start(f32[128,512]{1,0:T(8,128)S(1)} %multiply_add_fusion.8), channel_id=1, source_target_pairs={{0,4},{4,8},{8,12},{12,16},{16,20},{20,24},{24,28},{28,32},{32,36}... | collective-permute-start | bytes 786440 | tf_op jit(solution)/shard_map/while/body/eval_jaxpr/ppermute | solution.py:13
  266.3 9.8 %collective-permute-start.1 = (f32[128,512]{1,0:T(8,128)S(1)}, f32[128,512]{1,0:T(8,128)S(1)}, u32[]{:S(2)}, u32[]{:S(2)}) collective-permute-start(f32[128,512]{1,0:T(8,128)S(1)} %multiply_add_fusion.8), channel_id=1, source_target_pairs={{0,4},{4,8},{8,12},{12,16},{16,20},{20,24},{24,28},{28,32},{32,36}... | collective-permute-start | bytes 786440 | tf_op jit(solution)/shard_map/while/body/eval_jaxpr/ppermute | solution.py:13
  276.2 9.8 %collective-permute-start.1 = (f32[128,512]{1,0:T(8,128)S(1)}, f32[128,512]{1,0:T(8,128)S(1)}, u32[]{:S(2)}, u32[]{:S(2)}) collective-permute-start(f32[128,512]{1,0:T(8,128)S(1)} %multiply_add_fusion.8), channel_id=1, source_target_pairs={{0,4},{4,8},{8,12},{12,16},{16,20},{20,24},{24,28},{28,32},{32,36}... | collective-permute-start | bytes 786440 | tf_op jit(solution)/shard_map/while/body/eval_jaxpr/ppermute | solution.py:13
  286.1 9.8 %collective-permute-start.1 = (f32[128,512]{1,0:T(8,128)S(1)}, f32[128,512]{1,0:T(8,128)S(1)}, u32[]{:S(2)}, u32[]{:S(2)}) collective-permute-start(f32[128,512]{1,0:T(8,128)S(1)} %multiply_add_fusion.8), channel_id=1, source_target_pairs={{0,4},{4,8},{8,12},{12,16},{16,20},{20,24},{24,28},{28,32},{32,36}... | collective-permute-start | bytes 786440 | tf_op jit(solution)/shard_map/while/body/eval_jaxpr/ppermute | solution.py:13
  296.7 88.0 %reduce-scatter.2.cloned.1.call-start = ((), (), s32[]{:S(2)}) async-start(), calls=%async_computation.1 | async-start | bytes 2621440 | tf_op jit(solution)/shard_map/reduce_scatter | solution.py:60
  300.2 505.8 %all-reduce.6.cloned.1.call-start = ((), (), s32[]{:S(2)}) async-start(), calls=%async_computation.3 | async-start | bytes 4718592 | tf_op jit(solution)/shard_map/psum | solution.py:92
  387.5 7.9 collective-permute-start
  488.9 9.6 %collective-permute-start = (f32[128,512]{1,0:T(8,128)S(1)}, f32[128,512]{1,0:T(8,128)S(1)}, u32[]{:S(2)}, u32[]{:S(2)}) collective-permute-start(f32[128,512]{1,0:T(8,128)S(1)} %multiply_add_fusion.7), channel_id=1, source_target_pairs={{4,0},{8,4},{12,8},{16,12},{20,16},{24,20},{28,24},{32,28},{36,32}... | collective-permute-start | bytes 786440 | tf_op jit(solution)/shard_map/while/body/eval_jaxpr/ppermute | solution.py:13
  498.6 9.8 %collective-permute-start = (f32[128,512]{1,0:T(8,128)S(1)}, f32[128,512]{1,0:T(8,128)S(1)}, u32[]{:S(2)}, u32[]{:S(2)}) collective-permute-start(f32[128,512]{1,0:T(8,128)S(1)} %multiply_add_fusion.7), channel_id=1, source_target_pairs={{4,0},{8,4},{12,8},{16,12},{20,16},{24,20},{28,24},{32,28},{36,32}... | collective-permute-start | bytes 786440 | tf_op jit(solution)/shard_map/while/body/eval_jaxpr/ppermute | solution.py:13
  508.5 9.8 %collective-permute-start = (f32[128,512]{1,0:T(8,128)S(1)}, f32[128,512]{1,0:T(8,128)S(1)}, u32[]{:S(2)}, u32[]{:S(2)}) collective-permute-start(f32[128,512]{1,0:T(8,128)S(1)} %multiply_add_fusion.7), channel_id=1, source_target_pairs={{4,0},{8,4},{12,8},{16,12},{20,16},{24,20},{28,24},{32,28},{36,32}... | collective-permute-start | bytes 786440 | tf_op jit(solution)/shard_map/while/body/eval_jaxpr/ppermute | solution.py:13
  518.4 9.8 %collective-permute-start = (f32[128,512]{1,0:T(8,128)S(1)}, f32[128,512]{1,0:T(8,128)S(1)}, u32[]{:S(2)}, u32[]{:S(2)}) collective-permute-start(f32[128,512]{1,0:T(8,128)S(1)} %multiply_add_fusion.7), channel_id=1, source_target_pairs={{4,0},{8,4},{12,8},{16,12},{20,16},{24,20},{28,24},{32,28},{36,32}... | collective-permute-start | bytes 786440 | tf_op jit(solution)/shard_map/while/body/eval_jaxpr/ppermute | solution.py:13
  528.3 9.8 %collective-permute-start = (f32[128,512]{1,0:T(8,128)S(1)}, f32[128,512]{1,0:T(8,128)S(1)}, u32[]{:S(2)}, u32[]{:S(2)}) collective-permute-start(f32[128,512]{1,0:T(8,128)S(1)} %multiply_add_fusion.7), channel_id=1, source_target_pairs={{4,0},{8,4},{12,8},{16,12},{20,16},{24,20},{28,24},{32,28},{36,32}... | collective-permute-start | bytes 786440 | tf_op jit(solution)/shard_map/while/body/eval_jaxpr/ppermute | solution.py:13
  538.2 9.8 %collective-permute-start = (f32[128,512]{1,0:T(8,128)S(1)}, f32[128,512]{1,0:T(8,128)S(1)}, u32[]{:S(2)}, u32[]{:S(2)}) collective-permute-start(f32[128,512]{1,0:T(8,128)S(1)} %multiply_add_fusion.7), channel_id=1, source_target_pairs={{4,0},{8,4},{12,8},{16,12},{20,16},{24,20},{28,24},{32,28},{36,32}... | collective-permute-start | bytes 786440 | tf_op jit(solution)/shard_map/while/body/eval_jaxpr/ppermute | solution.py:13
  548.1 9.8 %collective-permute-start = (f32[128,512]{1,0:T(8,128)S(1)}, f32[128,512]{1,0:T(8,128)S(1)}, u32[]{:S(2)}, u32[]{:S(2)}) collective-permute-start(f32[128,512]{1,0:T(8,128)S(1)} %multiply_add_fusion.7), channel_id=1, source_target_pairs={{4,0},{8,4},{12,8},{16,12},{20,16},{24,20},{28,24},{32,28},{36,32}... | collective-permute-start | bytes 786440 | tf_op jit(solution)/shard_map/while/body/eval_jaxpr/ppermute | solution.py:13
  558.0 9.8 %collective-permute-start = (f32[128,512]{1,0:T(8,128)S(1)}, f32[128,512]{1,0:T(8,128)S(1)}, u32[]{:S(2)}, u32[]{:S(2)}) collective-permute-start(f32[128,512]{1,0:T(8,128)S(1)} %multiply_add_fusion.7), channel_id=1, source_target_pairs={{4,0},{8,4},{12,8},{16,12},{20,16},{24,20},{28,24},{32,28},{36,32}... | collective-permute-start | bytes 786440 | tf_op jit(solution)/shard_map/while/body/eval_jaxpr/ppermute | solution.py:13
  567.9 9.8 %collective-permute-start = (f32[128,512]{1,0:T(8,128)S(1)}, f32[128,512]{1,0:T(8,128)S(1)}, u32[]{:S(2)}, u32[]{:S(2)}) collective-permute-start(f32[128,512]{1,0:T(8,128)S(1)} %multiply_add_fusion.7), channel_id=1, source_target_pairs={{4,0},{8,4},{12,8},{16,12},{20,16},{24,20},{28,24},{32,28},{36,32}... | collective-permute-start | bytes 786440 | tf_op jit(solution)/shard_map/while/body/eval_jaxpr/ppermute | solution.py:13
  577.8 9.8 %collective-permute-start = (f32[128,512]{1,0:T(8,128)S(1)}, f32[128,512]{1,0:T(8,128)S(1)}, u32[]{:S(2)}, u32[]{:S(2)}) collective-permute-start(f32[128,512]{1,0:T(8,128)S(1)} %multiply_add_fusion.7), channel_id=1, source_target_pairs={{4,0},{8,4},{12,8},{16,12},{20,16},{24,20},{28,24},{32,28},{36,32}... | collective-permute-start | bytes 786440 | tf_op jit(solution)/shard_map/while/body/eval_jaxpr/ppermute | solution.py:13
  587.7 9.8 %collective-permute-start = (f32[128,512]{1,0:T(8,128)S(1)}, f32[128,512]{1,0:T(8,128)S(1)}, u32[]{:S(2)}, u32[]{:S(2)}) collective-permute-start(f32[128,512]{1,0:T(8,128)S(1)} %multiply_add_fusion.7), channel_id=1, source_target_pairs={{4,0},{8,4},{12,8},{16,12},{20,16},{24,20},{28,24},{32,28},{36,32}... | collective-permute-start | bytes 786440 | tf_op jit(solution)/shard_map/while/body/eval_jaxpr/ppermute | solution.py:13
  597.6 9.8 %collective-permute-start = (f32[128,512]{1,0:T(8,128)S(1)}, f32[128,512]{1,0:T(8,128)S(1)}, u32[]{:S(2)}, u32[]{:S(2)}) collective-permute-start(f32[128,512]{1,0:T(8,128)S(1)} %multiply_add_fusion.7), channel_id=1, source_target_pairs={{4,0},{8,4},{12,8},{16,12},{20,16},{24,20},{28,24},{32,28},{36,32}... | collective-permute-start | bytes 786440 | tf_op jit(solution)/shard_map/while/body/eval_jaxpr/ppermute | solution.py:13
  607.5 9.8 %collective-permute-start = (f32[128,512]{1,0:T(8,128)S(1)}, f32[128,512]{1,0:T(8,128)S(1)}, u32[]{:S(2)}, u32[]{:S(2)}) collective-permute-start(f32[128,512]{1,0:T(8,128)S(1)} %multiply_add_fusion.7), channel_id=1, source_target_pairs={{4,0},{8,4},{12,8},{16,12},{20,16},{24,20},{28,24},{32,28},{36,32}... | collective-permute-start | bytes 786440 | tf_op jit(solution)/shard_map/while/body/eval_jaxpr/ppermute | solution.py:13
  617.4 9.8 %collective-permute-start = (f32[128,512]{1,0:T(8,128)S(1)}, f32[128,512]{1,0:T(8,128)S(1)}, u32[]{:S(2)}, u32[]{:S(2)}) collective-permute-start(f32[128,512]{1,0:T(8,128)S(1)} %multiply_add_fusion.7), channel_id=1, source_target_pairs={{4,0},{8,4},{12,8},{16,12},{20,16},{24,20},{28,24},{32,28},{36,32}... | collective-permute-start | bytes 786440 | tf_op jit(solution)/shard_map/while/body/eval_jaxpr/ppermute | solution.py:13
  627.3 9.8 %collective-permute-start = (f32[128,512]{1,0:T(8,128)S(1)}, f32[128,512]{1,0:T(8,128)S(1)}, u32[]{:S(2)}, u32[]{:S(2)}) collective-permute-start(f32[128,512]{1,0:T(8,128)S(1)} %multiply_add_fusion.7), channel_id=1, source_target_pairs={{4,0},{8,4},{12,8},{16,12},{20,16},{24,20},{28,24},{32,28},{36,32}... | collective-permute-start | bytes 786440 | tf_op jit(solution)/shard_map/while/body/eval_jaxpr/ppermute | solution.py:13
  637.2 9.8 %collective-permute-start = (f32[128,512]{1,0:T(8,128)S(1)}, f32[128,512]{1,0:T(8,128)S(1)}, u32[]{:S(2)}, u32[]{:S(2)}) collective-permute-start(f32[128,512]{1,0:T(8,128)S(1)} %multiply_add_fusion.7), channel_id=1, source_target_pairs={{4,0},{8,4},{12,8},{16,12},{20,16},{24,20},{28,24},{32,28},{36,32}... | collective-permute-start | bytes 786440 | tf_op jit(solution)/shard_map/while/body/eval_jaxpr/ppermute | solution.py:13
  647.1 9.8 %collective-permute-start = (f32[128,512]{1,0:T(8,128)S(1)}, f32[128,512]{1,0:T(8,128)S(1)}, u32[]{:S(2)}, u32[]{:S(2)}) collective-permute-start(f32[128,512]{1,0:T(8,128)S(1)} %multiply_add_fusion.7), channel_id=1, source_target_pairs={{4,0},{8,4},{12,8},{16,12},{20,16},{24,20},{28,24},{32,28},{36,32}... | collective-permute-start | bytes 786440 | tf_op jit(solution)/shard_map/while/body/eval_jaxpr/ppermute | solution.py:13
  657.0 9.8 %collective-permute-start = (f32[128,512]{1,0:T(8,128)S(1)}, f32[128,512]{1,0:T(8,128)S(1)}, u32[]{:S(2)}, u32[]{:S(2)}) collective-permute-start(f32[128,512]{1,0:T(8,128)S(1)} %multiply_add_fusion.7), channel_id=1, source_target_pairs={{4,0},{8,4},{12,8},{16,12},{20,16},{24,20},{28,24},{32,28},{36,32}... | collective-permute-start | bytes 786440 | tf_op jit(solution)/shard_map/while/body/eval_jaxpr/ppermute | solution.py:13
  (25 other events, 725.1 us)
Sparse Core Ops, SparseCore 0:
  296.9 53.3 all-gather.1
  352.6 32.0 reduce-scatter.1
  671.7 134.1 all-reduce.5
where the time goes:
time: 820 us; the launch traced here: 818 us
  waiting for transfers between devices  525 us (64%)
  starting transfers between devices  230 us (28%)
  other arithmetic  24.4 us (3%)
  between operations  14.1 us (2%)
  matrix products  12.6 us (2%)
  local copies, waits for them, and re-layouts  9.91 us (1%)
    ppermute x62, waiting for transfers between devices, passed_along(): lax.ppermute(value, axis, [(source, source + steps) for source in range(f...  318 us
    ppermute x62, starting transfers between devices, passed_along(): lax.ppermute(value, axis, [(source, source + steps) for source in range(f...  230 us
    psum x1, waiting for transfers between devices, body(): grad_b, grad_c = lax.psum((grad_b_part, grad_c_part), 'tm')  134 us
    all_gather x1, waiting for transfers between devices, body(): lax.all_gather(states_bf, 'chan', axis=1, tiled=True)  49.7 us
    reduce_scatter x1, waiting for transfers between devices, body(): lax.psum_scatter(jnp.einsum('kup,fkus->pfs', kernel_c, cot_stack, preferr...  23.6 us
  transfers between devices with their start and end apart: 65, of which 65 were waited for; matrix products, arithmetic and copies ran while one was open for 2% of the time, Pallas kernels for 0%

commit v1 on v0

--- a/solution.py
+++ b/solution.py
@@ -85,7 +85,13 @@
     grad_b_part = jnp.einsum(
         "fps,fkcs->kpc", adjoint_bf, input_stack, preferred_element_type=jnp.float32
     )
-    shifted = stencil_stack(lax.all_gather(states_bf, "chan", axis=1, tiled=True), W, 1)
+    shifted = stencil_stack(
+        jnp.concatenate(
+            lax.all_to_all(jnp.stack([states_bf] * lax.axis_size("chan")), "chan", 0, 0), axis=1
+        ),
+        W,
+        1,
+    )
     grad_c_part = jnp.einsum(
         "fus,fkps->kup", cotangent, shifted, preferred_element_type=jnp.float32
     )

time: 820 us -> 791 us (0.965)
  waiting for transfers between devices: 525 us -> 493 us
    all_gather x1 -> x0, waiting for transfers between devices: 49.7 us -> none  [body(): lax.all_gather(states_bf, 'chan', axis=1, tiled=True)]
    ppermute x62, waiting for transfers between devices: 318 us -> 350 us  [passed_along(): lax.ppermute(value, axis, [(source, source + steps) for source in range(f...]
    reduce_scatter x1, waiting for transfers between devices: 23.6 us -> 0.01 us  [body(): lax.psum_scatter(jnp.einsum('kup,fkus->pfs', kernel_c, cot_stack, preferr...]
    all_to_all x0 -> x1, waiting for transfers between devices: none -> 9.72 us  [body(): lax.all_to_all(jnp.stack([states_bf] * lax.axis_size('chan')), 'chan', 0, 0)]
  transfers between devices with their start and end apart: 65 -> 65, of which waited for: 65 -> 64; matrix products, arithmetic and copies ran while one was open for 2% -> 2% of each run, Pallas kernels for 0% -> 0%
where the time goes in v1:
time: 791 us; the launch traced here: 788 us
  waiting for transfers between devices  493 us (62%)
  starting transfers between devices  234 us (30%)
  other arithmetic  22.6 us (3%)
  between operations  14.4 us (2%)
  matrix products  12.6 us (2%)
  local copies, waits for them, and re-layouts  11.1 us (1%)
    ppermute x62, waiting for transfers between devices, passed_along(): lax.ppermute(value, axis, [(source, source + steps) for source in range(f...  350 us
    ppermute x62, starting transfers between devices, passed_along(): lax.ppermute(value, axis, [(source, source + steps) for source in range(f...  229 us
    psum x1, waiting for transfers between devices, body(): grad_b, grad_c = lax.psum((grad_b_part, grad_c_part), 'tm')  133 us
  transfers between devices with their start and end apart: 65, of which 64 were waited for; matrix products, arithmetic and copies ran while one was open for 2% of the time, Pallas kernels for 0%

profile of v1, /device:TPU:1, one launch (start us, length us, event | category | flops | bytes accessed | tf_op | source)
XLA Modules:
  0.0 788.4 jit_solution(6736808904901830316)
XLA Ops:
  25.6 275.2 %while.51 = (s32[]{:T(128)}, f32[128,512]{1,0:T(8,128)S(1)}, f32[128]{0:T(128)S(1)}, f32[128,512]{1,0:T(8,128)S(1)}, s32[]{:T(128)}) while((s32[]{:T(128)}, f32[128,512]{1,0:T(8,128)S(1)}, f32[128]{0:T(128)S(1)}, f32[128,512]{1,0:T(8,128)S(1)}, s32[]{:T(128)}) %tuple.105), condition=%wide.region_12.13_spmd, body=%wide.region_11.12_spmd.sunk | while | flops 131074 | bytes 1835621 | solution.py:54
  152.4 6.5 collective-permute-start.1
  162.3 6.5 collective-permute-start.1
  172.2 6.5 collective-permute-start.1
  182.1 6.5 collective-permute-start.1
  192.0 6.5 collective-permute-start.1
  201.9 6.5 collective-permute-start.1
  211.8 6.5 collective-permute-start.1
  221.7 6.5 collective-permute-start.1
  231.6 6.5 collective-permute-start.1
  241.5 6.5 collective-permute-start.1
  251.4 6.5 collective-permute-start.1
  261.3 6.5 collective-permute-start.1
  271.2 6.5 collective-permute-start.1
  281.1 6.5 collective-permute-start.1
  291.0 6.5 collective-permute-start.1
  306.3 9.7 %all-to-all-done = bf16[4,2,128,512]{3,2,1,0:T(8,128)(2,1)S(1)} async-done(((bf16[4,2,128,512]{3,2,1,0:T(8,128)(2,1)}), bf16[4,2,128,512]{3,2,1,0:T(8,128)(2,1)S(1)}, u32[]{:S(2)}, u32[]{:S(2)}) %all-to-all-start) | async-done | bytes 1048608 | tf_op jit(solution)/shard_map/all_to_all | solution.py:90
  327.2 310.7 %while.50 = (s32[]{:T(128)}, f32[128,512]{1,0:T(8,128)S(1)}, f32[128]{0:T(128)S(1)}, f32[128,512]{1,0:T(8,128)S(1)}, s32[]{:T(128)}) while((s32[]{:T(128)}, f32[128,512]{1,0:T(8,128)S(1)}, f32[128]{0:T(128)S(1)}, f32[128,512]{1,0:T(8,128)S(1)}, s32[]{:T(128)}) %tuple.115), condition=%wide.region_6.7_spmd, body=%wide.region_5.6_spmd.sunk | while | flops 131074 | bytes 1835621 | solution.py:79
  329.3 10.0 %collective-permute-done = f32[128,512]{1,0:T(8,128)S(1)} collective-permute-done((f32[128,512]{1,0:T(8,128)S(1)}, f32[128,512]{1,0:T(8,128)S(1)}, u32[]{:S(2)}, u32[]{:S(2)}) %collective-permute-start) | collective-permute-done | bytes 262176 | tf_op jit(solution)/shard_map/while/body/eval_jaxpr/ppermute | solution.py:13
  341.3 6.3 collective-permute-done
  349.7 10.0 %collective-permute-done = f32[128,512]{1,0:T(8,128)S(1)} collective-permute-done((f32[128,512]{1,0:T(8,128)S(1)}, f32[128,512]{1,0:T(8,128)S(1)}, u32[]{:S(2)}, u32[]{:S(2)}) %collective-permute-start) | collective-permute-done | bytes 262176 | tf_op jit(solution)/shard_map/while/body/eval_jaxpr/ppermute | solution.py:13
  370.1 10.0 %collective-permute-done = f32[128,512]{1,0:T(8,128)S(1)} collective-permute-done((f32[128,512]{1,0:T(8,128)S(1)}, f32[128,512]{1,0:T(8,128)S(1)}, u32[]{:S(2)}, u32[]{:S(2)}) %collective-permute-start) | collective-permute-done | bytes 262176 | tf_op jit(solution)/shard_map/while/body/eval_jaxpr/ppermute | solution.py:13
  390.5 9.9 %collective-permute-done = f32[128,512]{1,0:T(8,128)S(1)} collective-permute-done((f32[128,512]{1,0:T(8,128)S(1)}, f32[128,512]{1,0:T(8,128)S(1)}, u32[]{:S(2)}, u32[]{:S(2)}) %collective-permute-start) | collective-permute-done | bytes 262176 | tf_op jit(solution)/shard_map/while/body/eval_jaxpr/ppermute | solution.py:13
  402.4 7.9 collective-permute-done
  412.3 7.9 collective-permute-done
  422.2 7.9 collective-permute-done
  432.1 7.9 collective-permute-done
  442.0 7.9 collective-permute-done
  451.9 7.9 collective-permute-done
  461.8 7.9 collective-permute-done
  471.7 7.9 collective-permute-done
  481.6 7.9 collective-permute-done
  491.5 7.9 collective-permute-done
  501.4 7.9 collective-permute-done
  511.3 7.9 collective-permute-done
  521.2 7.9 collective-permute-done
  531.1 7.9 collective-permute-done
  541.0 7.9 collective-permute-done
  550.9 7.9 collective-permute-done
  560.8 7.9 collective-permute-done
  570.7 7.9 collective-permute-done
  580.6 7.9 collective-permute-done
  590.5 7.9 collective-permute-done
  600.4 7.9 collective-permute-done
  610.3 7.9 collective-permute-done
  620.2 7.9 collective-permute-done
  630.0 7.9 collective-permute-done
  643.6 132.9 %all-reduce.6.cloned.1.call-done = (f32[9,128,256]{1,2,0:T(8,128)}, f32[9,64,512]{2,1,0:T(8,128)}) async-done(((f32[9,128,256]{1,2,0:T(8,128)}, f32[9,64,512]{2,1,0:T(8,128)}), (f32[9,128,256]{1,2,0:T(8,128)}, f32[9,64,512]{2,1,0:T(8,128)})) %all-reduce.6.cloned.1.call-update) | async-done | bytes 2359312 | tf_op jit(solution)/shard_map/psum | solution.py:98
  (234 shorter events, 300.4 us)
Async XLA Ops:
  7.2 317.3 %reduce-scatter.2.cloned.1.call-start = ((), (), s32[]{:S(2)}) async-start(), calls=%async_computation.2 | async-start | bytes 2621440 | tf_op jit(solution)/shard_map/reduce_scatter | solution.py:60
  143.0 9.3 %collective-permute-start.1 = (f32[128,512]{1,0:T(8,128)S(1)}, f32[128,512]{1,0:T(8,128)S(1)}, u32[]{:S(2)}, u32[]{:S(2)}) collective-permute-start(f32[128,512]{1,0:T(8,128)S(1)} %multiply_add_fusion.8), channel_id=1, source_target_pairs={{0,4},{4,8},{8,12},{12,16},{16,20},{20,24},{24,28},{28,32},{32,36}... | collective-permute-start | bytes 786440 | tf_op jit(solution)/shard_map/while/body/eval_jaxpr/ppermute | solution.py:13
  152.4 9.8 %collective-permute-start.1 = (f32[128,512]{1,0:T(8,128)S(1)}, f32[128,512]{1,0:T(8,128)S(1)}, u32[]{:S(2)}, u32[]{:S(2)}) collective-permute-start(f32[128,512]{1,0:T(8,128)S(1)} %multiply_add_fusion.8), channel_id=1, source_target_pairs={{0,4},{4,8},{8,12},{12,16},{16,20},{20,24},{24,28},{28,32},{32,36}... | collective-permute-start | bytes 786440 | tf_op jit(solution)/shard_map/while/body/eval_jaxpr/ppermute | solution.py:13
  162.3 9.8 %collective-permute-start.1 = (f32[128,512]{1,0:T(8,128)S(1)}, f32[128,512]{1,0:T(8,128)S(1)}, u32[]{:S(2)}, u32[]{:S(2)}) collective-permute-start(f32[128,512]{1,0:T(8,128)S(1)} %multiply_add_fusion.8), channel_id=1, source_target_pairs={{0,4},{4,8},{8,12},{12,16},{16,20},{20,24},{24,28},{28,32},{32,36}... | collective-permute-start | bytes 786440 | tf_op jit(solution)/shard_map/while/body/eval_jaxpr/ppermute | solution.py:13
  172.2 9.8 %collective-permute-start.1 = (f32[128,512]{1,0:T(8,128)S(1)}, f32[128,512]{1,0:T(8,128)S(1)}, u32[]{:S(2)}, u32[]{:S(2)}) collective-permute-start(f32[128,512]{1,0:T(8,128)S(1)} %multiply_add_fusion.8), channel_id=1, source_target_pairs={{0,4},{4,8},{8,12},{12,16},{16,20},{20,24},{24,28},{28,32},{32,36}... | collective-permute-start | bytes 786440 | tf_op jit(solution)/shard_map/while/body/eval_jaxpr/ppermute | solution.py:13
  182.1 9.8 %collective-permute-start.1 = (f32[128,512]{1,0:T(8,128)S(1)}, f32[128,512]{1,0:T(8,128)S(1)}, u32[]{:S(2)}, u32[]{:S(2)}) collective-permute-start(f32[128,512]{1,0:T(8,128)S(1)} %multiply_add_fusion.8), channel_id=1, source_target_pairs={{0,4},{4,8},{8,12},{12,16},{16,20},{20,24},{24,28},{28,32},{32,36}... | collective-permute-start | bytes 786440 | tf_op jit(solution)/shard_map/while/body/eval_jaxpr/ppermute | solution.py:13
  192.0 9.8 %collective-permute-start.1 = (f32[128,512]{1,0:T(8,128)S(1)}, f32[128,512]{1,0:T(8,128)S(1)}, u32[]{:S(2)}, u32[]{:S(2)}) collective-permute-start(f32[128,512]{1,0:T(8,128)S(1)} %multiply_add_fusion.8), channel_id=1, source_target_pairs={{0,4},{4,8},{8,12},{12,16},{16,20},{20,24},{24,28},{28,32},{32,36}... | collective-permute-start | bytes 786440 | tf_op jit(solution)/shard_map/while/body/eval_jaxpr/ppermute | solution.py:13
  201.9 9.8 %collective-permute-start.1 = (f32[128,512]{1,0:T(8,128)S(1)}, f32[128,512]{1,0:T(8,128)S(1)}, u32[]{:S(2)}, u32[]{:S(2)}) collective-permute-start(f32[128,512]{1,0:T(8,128)S(1)} %multiply_add_fusion.8), channel_id=1, source_target_pairs={{0,4},{4,8},{8,12},{12,16},{16,20},{20,24},{24,28},{28,32},{32,36}... | collective-permute-start | bytes 786440 | tf_op jit(solution)/shard_map/while/body/eval_jaxpr/ppermute | solution.py:13
  211.8 9.8 %collective-permute-start.1 = (f32[128,512]{1,0:T(8,128)S(1)}, f32[128,512]{1,0:T(8,128)S(1)}, u32[]{:S(2)}, u32[]{:S(2)}) collective-permute-start(f32[128,512]{1,0:T(8,128)S(1)} %multiply_add_fusion.8), channel_id=1, source_target_pairs={{0,4},{4,8},{8,12},{12,16},{16,20},{20,24},{24,28},{28,32},{32,36}... | collective-permute-start | bytes 786440 | tf_op jit(solution)/shard_map/while/body/eval_jaxpr/ppermute | solution.py:13
  221.7 9.8 %collective-permute-start.1 = (f32[128,512]{1,0:T(8,128)S(1)}, f32[128,512]{1,0:T(8,128)S(1)}, u32[]{:S(2)}, u32[]{:S(2)}) collective-permute-start(f32[128,512]{1,0:T(8,128)S(1)} %multiply_add_fusion.8), channel_id=1, source_target_pairs={{0,4},{4,8},{8,12},{12,16},{16,20},{20,24},{24,28},{28,32},{32,36}... | collective-permute-start | bytes 786440 | tf_op jit(solution)/shard_map/while/body/eval_jaxpr/ppermute | solution.py:13
  231.6 9.8 %collective-permute-start.1 = (f32[128,512]{1,0:T(8,128)S(1)}, f32[128,512]{1,0:T(8,128)S(1)}, u32[]{:S(2)}, u32[]{:S(2)}) collective-permute-start(f32[128,512]{1,0:T(8,128)S(1)} %multiply_add_fusion.8), channel_id=1, source_target_pairs={{0,4},{4,8},{8,12},{12,16},{16,20},{20,24},{24,28},{28,32},{32,36}... | collective-permute-start | bytes 786440 | tf_op jit(solution)/shard_map/while/body/eval_jaxpr/ppermute | solution.py:13
  241.5 9.8 %collective-permute-start.1 = (f32[128,512]{1,0:T(8,128)S(1)}, f32[128,512]{1,0:T(8,128)S(1)}, u32[]{:S(2)}, u32[]{:S(2)}) collective-permute-start(f32[128,512]{1,0:T(8,128)S(1)} %multiply_add_fusion.8), channel_id=1, source_target_pairs={{0,4},{4,8},{8,12},{12,16},{16,20},{20,24},{24,28},{28,32},{32,36}... | collective-permute-start | bytes 786440 | tf_op jit(solution)/shard_map/while/body/eval_jaxpr/ppermute | solution.py:13
  251.4 9.8 %collective-permute-start.1 = (f32[128,512]{1,0:T(8,128)S(1)}, f32[128,512]{1,0:T(8,128)S(1)}, u32[]{:S(2)}, u32[]{:S(2)}) collective-permute-start(f32[128,512]{1,0:T(8,128)S(1)} %multiply_add_fusion.8), channel_id=1, source_target_pairs={{0,4},{4,8},{8,12},{12,16},{16,20},{20,24},{24,28},{28,32},{32,36}... | collective-permute-start | bytes 786440 | tf_op jit(solution)/shard_map/while/body/eval_jaxpr/ppermute | solution.py:13
  261.3 9.8 %collective-permute-start.1 = (f32[128,512]{1,0:T(8,128)S(1)}, f32[128,512]{1,0:T(8,128)S(1)}, u32[]{:S(2)}, u32[]{:S(2)}) collective-permute-start(f32[128,512]{1,0:T(8,128)S(1)} %multiply_add_fusion.8), channel_id=1, source_target_pairs={{0,4},{4,8},{8,12},{12,16},{16,20},{20,24},{24,28},{28,32},{32,36}... | collective-permute-start | bytes 786440 | tf_op jit(solution)/shard_map/while/body/eval_jaxpr/ppermute | solution.py:13
  271.2 9.8 %collective-permute-start.1 = (f32[128,512]{1,0:T(8,128)S(1)}, f32[128,512]{1,0:T(8,128)S(1)}, u32[]{:S(2)}, u32[]{:S(2)}) collective-permute-start(f32[128,512]{1,0:T(8,128)S(1)} %multiply_add_fusion.8), channel_id=1, source_target_pairs={{0,4},{4,8},{8,12},{12,16},{16,20},{20,24},{24,28},{28,32},{32,36}... | collective-permute-start | bytes 786440 | tf_op jit(solution)/shard_map/while/body/eval_jaxpr/ppermute | solution.py:13
  281.1 9.8 %collective-permute-start.1 = (f32[128,512]{1,0:T(8,128)S(1)}, f32[128,512]{1,0:T(8,128)S(1)}, u32[]{:S(2)}, u32[]{:S(2)}) collective-permute-start(f32[128,512]{1,0:T(8,128)S(1)} %multiply_add_fusion.8), channel_id=1, source_target_pairs={{0,4},{4,8},{8,12},{12,16},{16,20},{20,24},{24,28},{28,32},{32,36}... | collective-permute-start | bytes 786440 | tf_op jit(solution)/shard_map/while/body/eval_jaxpr/ppermute | solution.py:13
  291.0 9.8 %collective-permute-start.1 = (f32[128,512]{1,0:T(8,128)S(1)}, f32[128,512]{1,0:T(8,128)S(1)}, u32[]{:S(2)}, u32[]{:S(2)}) collective-permute-start(f32[128,512]{1,0:T(8,128)S(1)} %multiply_add_fusion.8), channel_id=1, source_target_pairs={{0,4},{4,8},{8,12},{12,16},{16,20},{20,24},{24,28},{28,32},{32,36}... | collective-permute-start | bytes 786440 | tf_op jit(solution)/shard_map/while/body/eval_jaxpr/ppermute | solution.py:13
  302.0 14.1 %all-to-all-start = ((bf16[4,2,128,512]{3,2,1,0:T(8,128)(2,1)}), bf16[4,2,128,512]{3,2,1,0:T(8,128)(2,1)S(1)}, u32[]{:S(2)}, u32[]{:S(2)}) async-start(bf16[4,2,128,512]{3,2,1,0:T(8,128)(2,1)} %stack.115), calls=%async_computation.1 | async-start | bytes 2097152 | tf_op jit(solution)/shard_map/all_to_all | solution.py:90
  306.2 470.3 %all-reduce.6.cloned.1.call-start = ((), (), s32[]{:S(2)}) async-start(), calls=%async_computation.3 | async-start | bytes 4718592 | tf_op jit(solution)/shard_map/psum | solution.py:98
  327.3 12.0 %collective-permute-start = (f32[128,512]{1,0:T(8,128)S(1)}, f32[128,512]{1,0:T(8,128)S(1)}, u32[]{:S(2)}, u32[]{:S(2)}) collective-permute-start(f32[128,512]{1,0:T(8,128)S(1)} %multiply_add_fusion.7), channel_id=1, source_target_pairs={{4,0},{8,4},{12,8},{16,12},{20,16},{24,20},{28,24},{32,28},{36,32}... | collective-permute-start | bytes 786440 | tf_op jit(solution)/shard_map/while/body/eval_jaxpr/ppermute | solution.py:13
  339.4 8.2 %collective-permute-start = (f32[128,512]{1,0:T(8,128)S(1)}, f32[128,512]{1,0:T(8,128)S(1)}, u32[]{:S(2)}, u32[]{:S(2)}) collective-permute-start(f32[128,512]{1,0:T(8,128)S(1)} %multiply_add_fusion.7), channel_id=1, source_target_pairs={{4,0},{8,4},{12,8},{16,12},{20,16},{24,20},{28,24},{32,28},{36,32}... | collective-permute-start | bytes 786440 | tf_op jit(solution)/shard_map/while/body/eval_jaxpr/ppermute | solution.py:13
  347.7 12.0 %collective-permute-start = (f32[128,512]{1,0:T(8,128)S(1)}, f32[128,512]{1,0:T(8,128)S(1)}, u32[]{:S(2)}, u32[]{:S(2)}) collective-permute-start(f32[128,512]{1,0:T(8,128)S(1)} %multiply_add_fusion.7), channel_id=1, source_target_pairs={{4,0},{8,4},{12,8},{16,12},{20,16},{24,20},{28,24},{32,28},{36,32}... | collective-permute-start | bytes 786440 | tf_op jit(solution)/shard_map/while/body/eval_jaxpr/ppermute | solution.py:13
  368.2 12.0 %collective-permute-start = (f32[128,512]{1,0:T(8,128)S(1)}, f32[128,512]{1,0:T(8,128)S(1)}, u32[]{:S(2)}, u32[]{:S(2)}) collective-permute-start(f32[128,512]{1,0:T(8,128)S(1)} %multiply_add_fusion.7), channel_id=1, source_target_pairs={{4,0},{8,4},{12,8},{16,12},{20,16},{24,20},{28,24},{32,28},{36,32}... | collective-permute-start | bytes 786440 | tf_op jit(solution)/shard_map/while/body/eval_jaxpr/ppermute | solution.py:13
  388.6 11.9 %collective-permute-start = (f32[128,512]{1,0:T(8,128)S(1)}, f32[128,512]{1,0:T(8,128)S(1)}, u32[]{:S(2)}, u32[]{:S(2)}) collective-permute-start(f32[128,512]{1,0:T(8,128)S(1)} %multiply_add_fusion.7), channel_id=1, source_target_pairs={{4,0},{8,4},{12,8},{16,12},{20,16},{24,20},{28,24},{32,28},{36,32}... | collective-permute-start | bytes 786440 | tf_op jit(solution)/shard_map/while/body/eval_jaxpr/ppermute | solution.py:13
  400.5 9.8 %collective-permute-start = (f32[128,512]{1,0:T(8,128)S(1)}, f32[128,512]{1,0:T(8,128)S(1)}, u32[]{:S(2)}, u32[]{:S(2)}) collective-permute-start(f32[128,512]{1,0:T(8,128)S(1)} %multiply_add_fusion.7), channel_id=1, source_target_pairs={{4,0},{8,4},{12,8},{16,12},{20,16},{24,20},{28,24},{32,28},{36,32}... | collective-permute-start | bytes 786440 | tf_op jit(solution)/shard_map/while/body/eval_jaxpr/ppermute | solution.py:13
  410.4 9.8 %collective-permute-start = (f32[128,512]{1,0:T(8,128)S(1)}, f32[128,512]{1,0:T(8,128)S(1)}, u32[]{:S(2)}, u32[]{:S(2)}) collective-permute-start(f32[128,512]{1,0:T(8,128)S(1)} %multiply_add_fusion.7), channel_id=1, source_target_pairs={{4,0},{8,4},{12,8},{16,12},{20,16},{24,20},{28,24},{32,28},{36,32}... | collective-permute-start | bytes 786440 | tf_op jit(solution)/shard_map/while/body/eval_jaxpr/ppermute | solution.py:13
  420.3 9.8 %collective-permute-start = (f32[128,512]{1,0:T(8,128)S(1)}, f32[128,512]{1,0:T(8,128)S(1)}, u32[]{:S(2)}, u32[]{:S(2)}) collective-permute-start(f32[128,512]{1,0:T(8,128)S(1)} %multiply_add_fusion.7), channel_id=1, source_target_pairs={{4,0},{8,4},{12,8},{16,12},{20,16},{24,20},{28,24},{32,28},{36,32}... | collective-permute-start | bytes 786440 | tf_op jit(solution)/shard_map/while/body/eval_jaxpr/ppermute | solution.py:13
  430.2 9.8 %collective-permute-start = (f32[128,512]{1,0:T(8,128)S(1)}, f32[128,512]{1,0:T(8,128)S(1)}, u32[]{:S(2)}, u32[]{:S(2)}) collective-permute-start(f32[128,512]{1,0:T(8,128)S(1)} %multiply_add_fusion.7), channel_id=1, source_target_pairs={{4,0},{8,4},{12,8},{16,12},{20,16},{24,20},{28,24},{32,28},{36,32}... | collective-permute-start | bytes 786440 | tf_op jit(solution)/shard_map/while/body/eval_jaxpr/ppermute | solution.py:13
  440.1 9.8 %collective-permute-start = (f32[128,512]{1,0:T(8,128)S(1)}, f32[128,512]{1,0:T(8,128)S(1)}, u32[]{:S(2)}, u32[]{:S(2)}) collective-permute-start(f32[128,512]{1,0:T(8,128)S(1)} %multiply_add_fusion.7), channel_id=1, source_target_pairs={{4,0},{8,4},{12,8},{16,12},{20,16},{24,20},{28,24},{32,28},{36,32}... | collective-permute-start | bytes 786440 | tf_op jit(solution)/shard_map/while/body/eval_jaxpr/ppermute | solution.py:13
  450.0 9.8 %collective-permute-start = (f32[128,512]{1,0:T(8,128)S(1)}, f32[128,512]{1,0:T(8,128)S(1)}, u32[]{:S(2)}, u32[]{:S(2)}) collective-permute-start(f32[128,512]{1,0:T(8,128)S(1)} %multiply_add_fusion.7), channel_id=1, source_target_pairs={{4,0},{8,4},{12,8},{16,12},{20,16},{24,20},{28,24},{32,28},{36,32}... | collective-permute-start | bytes 786440 | tf_op jit(solution)/shard_map/while/body/eval_jaxpr/ppermute | solution.py:13
  459.9 9.8 %collective-permute-start = (f32[128,512]{1,0:T(8,128)S(1)}, f32[128,512]{1,0:T(8,128)S(1)}, u32[]{:S(2)}, u32[]{:S(2)}) collective-permute-start(f32[128,512]{1,0:T(8,128)S(1)} %multiply_add_fusion.7), channel_id=1, source_target_pairs={{4,0},{8,4},{12,8},{16,12},{20,16},{24,20},{28,24},{32,28},{36,32}... | collective-permute-start | bytes 786440 | tf_op jit(solution)/shard_map/while/body/eval_jaxpr/ppermute | solution.py:13
  469.8 9.8 %collective-permute-start = (f32[128,512]{1,0:T(8,128)S(1)}, f32[128,512]{1,0:T(8,128)S(1)}, u32[]{:S(2)}, u32[]{:S(2)}) collective-permute-start(f32[128,512]{1,0:T(8,128)S(1)} %multiply_add_fusion.7), channel_id=1, source_target_pairs={{4,0},{8,4},{12,8},{16,12},{20,16},{24,20},{28,24},{32,28},{36,32}... | collective-permute-start | bytes 786440 | tf_op jit(solution)/shard_map/while/body/eval_jaxpr/ppermute | solution.py:13
  479.7 9.8 %collective-permute-start = (f32[128,512]{1,0:T(8,128)S(1)}, f32[128,512]{1,0:T(8,128)S(1)}, u32[]{:S(2)}, u32[]{:S(2)}) collective-permute-start(f32[128,512]{1,0:T(8,128)S(1)} %multiply_add_fusion.7), channel_id=1, source_target_pairs={{4,0},{8,4},{12,8},{16,12},{20,16},{24,20},{28,24},{32,28},{36,32}... | collective-permute-start | bytes 786440 | tf_op jit(solution)/shard_map/while/body/eval_jaxpr/ppermute | solution.py:13
  489.6 9.8 %collective-permute-start = (f32[128,512]{1,0:T(8,128)S(1)}, f32[128,512]{1,0:T(8,128)S(1)}, u32[]{:S(2)}, u32[]{:S(2)}) collective-permute-start(f32[128,512]{1,0:T(8,128)S(1)} %multiply_add_fusion.7), channel_id=1, source_target_pairs={{4,0},{8,4},{12,8},{16,12},{20,16},{24,20},{28,24},{32,28},{36,32}... | collective-permute-start | bytes 786440 | tf_op jit(solution)/shard_map/while/body/eval_jaxpr/ppermute | solution.py:13
  499.5 9.8 %collective-permute-start = (f32[128,512]{1,0:T(8,128)S(1)}, f32[128,512]{1,0:T(8,128)S(1)}, u32[]{:S(2)}, u32[]{:S(2)}) collective-permute-start(f32[128,512]{1,0:T(8,128)S(1)} %multiply_add_fusion.7), channel_id=1, source_target_pairs={{4,0},{8,4},{12,8},{16,12},{20,16},{24,20},{28,24},{32,28},{36,32}... | collective-permute-start | bytes 786440 | tf_op jit(solution)/shard_map/while/body/eval_jaxpr/ppermute | solution.py:13
  509.4 9.8 %collective-permute-start = (f32[128,512]{1,0:T(8,128)S(1)}, f32[128,512]{1,0:T(8,128)S(1)}, u32[]{:S(2)}, u32[]{:S(2)}) collective-permute-start(f32[128,512]{1,0:T(8,128)S(1)} %multiply_add_fusion.7), channel_id=1, source_target_pairs={{4,0},{8,4},{12,8},{16,12},{20,16},{24,20},{28,24},{32,28},{36,32}... | collective-permute-start | bytes 786440 | tf_op jit(solution)/shard_map/while/body/eval_jaxpr/ppermute | solution.py:13
  519.3 9.8 %collective-permute-start = (f32[128,512]{1,0:T(8,128)S(1)}, f32[128,512]{1,0:T(8,128)S(1)}, u32[]{:S(2)}, u32[]{:S(2)}) collective-permute-start(f32[128,512]{1,0:T(8,128)S(1)} %multiply_add_fusion.7), channel_id=1, source_target_pairs={{4,0},{8,4},{12,8},{16,12},{20,16},{24,20},{28,24},{32,28},{36,32}... | collective-permute-start | bytes 786440 | tf_op jit(solution)/shard_map/while/body/eval_jaxpr/ppermute | solution.py:13
  529.2 9.8 %collective-permute-start = (f32[128,512]{1,0:T(8,128)S(1)}, f32[128,512]{1,0:T(8,128)S(1)}, u32[]{:S(2)}, u32[]{:S(2)}) collective-permute-start(f32[128,512]{1,0:T(8,128)S(1)} %multiply_add_fusion.7), channel_id=1, source_target_pairs={{4,0},{8,4},{12,8},{16,12},{20,16},{24,20},{28,24},{32,28},{36,32}... | collective-permute-start | bytes 786440 | tf_op jit(solution)/shard_map/while/body/eval_jaxpr/ppermute | solution.py:13
  539.1 9.8 %collective-permute-start = (f32[128,512]{1,0:T(8,128)S(1)}, f32[128,512]{1,0:T(8,128)S(1)}, u32[]{:S(2)}, u32[]{:S(2)}) collective-permute-start(f32[128,512]{1,0:T(8,128)S(1)} %multiply_add_fusion.7), channel_id=1, source_target_pairs={{4,0},{8,4},{12,8},{16,12},{20,16},{24,20},{28,24},{32,28},{36,32}... | collective-permute-start | bytes 786440 | tf_op jit(solution)/shard_map/while/body/eval_jaxpr/ppermute | solution.py:13
  549.0 9.8 %collective-permute-start = (f32[128,512]{1,0:T(8,128)S(1)}, f32[128,512]{1,0:T(8,128)S(1)}, u32[]{:S(2)}, u32[]{:S(2)}) collective-permute-start(f32[128,512]{1,0:T(8,128)S(1)} %multiply_add_fusion.7), channel_id=1, source_target_pairs={{4,0},{8,4},{12,8},{16,12},{20,16},{24,20},{28,24},{32,28},{36,32}... | collective-permute-start | bytes 786440 | tf_op jit(solution)/shard_map/while/body/eval_jaxpr/ppermute | solution.py:13
  558.8 9.8 %collective-permute-start = (f32[128,512]{1,0:T(8,128)S(1)}, f32[128,512]{1,0:T(8,128)S(1)}, u32[]{:S(2)}, u32[]{:S(2)}) collective-permute-start(f32[128,512]{1,0:T(8,128)S(1)} %multiply_add_fusion.7), channel_id=1, source_target_pairs={{4,0},{8,4},{12,8},{16,12},{20,16},{24,20},{28,24},{32,28},{36,32}... | collective-permute-start | bytes 786440 | tf_op jit(solution)/shard_map/while/body/eval_jaxpr/ppermute | solution.py:13
  568.7 9.8 %collective-permute-start = (f32[128,512]{1,0:T(8,128)S(1)}, f32[128,512]{1,0:T(8,128)S(1)}, u32[]{:S(2)}, u32[]{:S(2)}) collective-permute-start(f32[128,512]{1,0:T(8,128)S(1)} %multiply_add_fusion.7), channel_id=1, source_target_pairs={{4,0},{8,4},{12,8},{16,12},{20,16},{24,20},{28,24},{32,28},{36,32}... | collective-permute-start | bytes 786440 | tf_op jit(solution)/shard_map/while/body/eval_jaxpr/ppermute | solution.py:13
  578.6 9.8 %collective-permute-start = (f32[128,512]{1,0:T(8,128)S(1)}, f32[128,512]{1,0:T(8,128)S(1)}, u32[]{:S(2)}, u32[]{:S(2)}) collective-permute-start(f32[128,512]{1,0:T(8,128)S(1)} %multiply_add_fusion.7), channel_id=1, source_target_pairs={{4,0},{8,4},{12,8},{16,12},{20,16},{24,20},{28,24},{32,28},{36,32}... | collective-permute-start | bytes 786440 | tf_op jit(solution)/shard_map/while/body/eval_jaxpr/ppermute | solution.py:13
  588.5 9.8 %collective-permute-start = (f32[128,512]{1,0:T(8,128)S(1)}, f32[128,512]{1,0:T(8,128)S(1)}, u32[]{:S(2)}, u32[]{:S(2)}) collective-permute-start(f32[128,512]{1,0:T(8,128)S(1)} %multiply_add_fusion.7), channel_id=1, source_target_pairs={{4,0},{8,4},{12,8},{16,12},{20,16},{24,20},{28,24},{32,28},{36,32}... | collective-permute-start | bytes 786440 | tf_op jit(solution)/shard_map/while/body/eval_jaxpr/ppermute | solution.py:13
  598.4 9.8 %collective-permute-start = (f32[128,512]{1,0:T(8,128)S(1)}, f32[128,512]{1,0:T(8,128)S(1)}, u32[]{:S(2)}, u32[]{:S(2)}) collective-permute-start(f32[128,512]{1,0:T(8,128)S(1)} %multiply_add_fusion.7), channel_id=1, source_target_pairs={{4,0},{8,4},{12,8},{16,12},{20,16},{24,20},{28,24},{32,28},{36,32}... | collective-permute-start | bytes 786440 | tf_op jit(solution)/shard_map/while/body/eval_jaxpr/ppermute | solution.py:13
  608.3 9.8 %collective-permute-start = (f32[128,512]{1,0:T(8,128)S(1)}, f32[128,512]{1,0:T(8,128)S(1)}, u32[]{:S(2)}, u32[]{:S(2)}) collective-permute-start(f32[128,512]{1,0:T(8,128)S(1)} %multiply_add_fusion.7), channel_id=1, source_target_pairs={{4,0},{8,4},{12,8},{16,12},{20,16},{24,20},{28,24},{32,28},{36,32}... | collective-permute-start | bytes 786440 | tf_op jit(solution)/shard_map/while/body/eval_jaxpr/ppermute | solution.py:13
  618.2 9.8 %collective-permute-start = (f32[128,512]{1,0:T(8,128)S(1)}, f32[128,512]{1,0:T(8,128)S(1)}, u32[]{:S(2)}, u32[]{:S(2)}) collective-permute-start(f32[128,512]{1,0:T(8,128)S(1)} %multiply_add_fusion.7), channel_id=1, source_target_pairs={{4,0},{8,4},{12,8},{16,12},{20,16},{24,20},{28,24},{32,28},{36,32}... | collective-permute-start | bytes 786440 | tf_op jit(solution)/shard_map/while/body/eval_jaxpr/ppermute | solution.py:13
  628.1 9.8 %collective-permute-start = (f32[128,512]{1,0:T(8,128)S(1)}, f32[128,512]{1,0:T(8,128)S(1)}, u32[]{:S(2)}, u32[]{:S(2)}) collective-permute-start(f32[128,512]{1,0:T(8,128)S(1)} %multiply_add_fusion.7), channel_id=1, source_target_pairs={{4,0},{8,4},{12,8},{16,12},{20,16},{24,20},{28,24},{32,28},{36,32}... | collective-permute-start | bytes 786440 | tf_op jit(solution)/shard_map/while/body/eval_jaxpr/ppermute | solution.py:13
  (24 other events, 436.0 us)
Sparse Core Ops, SparseCore 0:
  19.0 32.8 reduce-scatter.1
  642.9 133.5 all-reduce.5
